TPU v7x, 128 devices: a whole 4x4x4 slice. The times are simulated.
128 devices in a mesh: ctx: 16 (over x_lo, z, core), tp: 8 (over y, x_hi).
Axes of the slice: x: 4 (x_hi: 2, x_lo: 2; x = x_hi * 2 + x_lo), y: 4, z: 4, core: 2. Of those that a mesh axis runs over, the one named last changes fastest.
Arguments:
- queries: bfloat16 [8192, 4096], P('ctx', 'tp'), may hold values from -6 to 6
- key_rows: bfloat16 [8192, 4096], P('ctx', 'tp'), may hold values from -6 to 6
- value_rows: bfloat16 [8192, 4096], P('ctx', 'tp'), may hold values from -30 to 30
- selection: int32 [16, 3], replicated, may hold values from 0 to 15, as said below
- out_weight: bfloat16 [4096, 7168], P('tp'), may hold values from -0.125 to 0.125
Outputs:
- mixed: bfloat16 [8192, 7168], P('ctx', 'tp')
Inputs may be any that keep to these rules, and one draw needn't show every extreme that they name: Row q of selection lists q first, then 3 - 1 distinct blocks below q; where fewer than that lie below q, the remaining entries are q.
All inputs are finite; a program needn't handle non-finite values.
Results may differ from a plain program's by a relative error of at most 0.013.
Values may be sent and summed in bfloat16 or wider, within the bound.
No kernel may reach another device: no remote copies, remote signals or barrier semaphores. Data moves between devices by JAX's collectives and lax.ppermute only.
A program may use at most 192 MiB of HBM per device.

v0:
```python
import jax
import jax.numpy as jnp
from jax import lax
from jax.sharding import PartitionSpec as P

HD = 128
BLOCK = 512
neg_fill = -1e30


def per_device(queries, key_rows, value_rows, selection, out_weight):
    row_count, feat_width = queries.shape
    head_count = feat_width // HD
    topk = selection.shape[1]
    ctx_place = lax.axis_index("ctx")
    first_row = ctx_place * row_count
    scaling = 1.0 / jnp.sqrt(jnp.float32(HD))
    query_heads = queries.reshape(row_count, head_count, HD).transpose(1, 0, 2)
    own_choice = lax.dynamic_slice_in_dim(selection, ctx_place, 1, 0)[0]
    usable = jnp.concatenate([jnp.ones((1,), bool), own_choice[1:] != own_choice[0]])
    kv_piece = lax.all_gather(
        jnp.concatenate([key_rows, value_rows], axis=1), "ctx", axis=0, tiled=True
    )
    picked = jnp.stack(
        [lax.dynamic_slice_in_dim(kv_piece, own_choice[s] * BLOCK, BLOCK, 0) for s in range(topk)]
    ).reshape(topk * BLOCK, 2, head_count, HD)
    key_heads = picked[:, 0].transpose(1, 0, 2)
    value_heads = picked[:, 1].transpose(1, 0, 2)
    query_pos = first_row + jnp.arange(row_count, dtype=jnp.int32)
    key_pos = (own_choice[:, None] * BLOCK + jnp.arange(BLOCK, dtype=jnp.int32)[None, :]).reshape(
        -1
    )
    slot_ok = jnp.repeat(usable, BLOCK)
    allowed = (key_pos[None, :] <= query_pos[:, None]) & slot_ok[None, :]
    scores = (
        jnp.einsum("htd,hsd->hts", query_heads, key_heads, preferred_element_type=jnp.float32)
        * scaling
    )
    run_max = jnp.max(jnp.where(allowed[None], scores, neg_fill), axis=-1)
    expo = jnp.where(allowed[None], jnp.exp(scores - run_max[..., None]), 0.0)
    run_sum = jnp.sum(expo, axis=-1)
    weights = expo.astype(jnp.bfloat16)
    run_acc = jnp.einsum("hts,hsd->htd", weights, value_heads, preferred_element_type=jnp.float32)
    attended = (
        (run_acc / run_sum[..., None])
        .astype(jnp.bfloat16)
        .transpose(1, 0, 2)
        .reshape(row_count, feat_width)
    )
    shares = lax.psum_scatter(
        lax.dot_general(
            out_weight, attended, (((0,), (1,)), ((), ())), preferred_element_type=jnp.float32
        ).astype(jnp.bfloat16),
        "tp",
        scatter_dimension=0,
        tiled=True,
    ).astype(jnp.float32)
    mixed_out = jnp.transpose(shares)
    return mixed_out.astype(jnp.bfloat16)


def solution(mesh):
    placed = (P("ctx", "tp"), P("ctx", "tp"), P("ctx", "tp"), P(), P("tp", None))
    return jax.shard_map(
        per_device, mesh=mesh, in_specs=placed, out_specs=P("ctx", "tp"), check_vma=False
    )
```

profile of v0, /device:TPU:1, one launch (start us, length us, event | category | flops | bytes accessed | tf_op | source)
XLA Modules:
  0.0 271.5 jit_solution(3721377676455916608)
XLA Ops:
  6.5 0.0 copy-start
  6.5 0.0 all-gather.2.cloned.1.call-start
  6.5 2.4 pad_maximum_fusion.1
  8.9 0.0 all-gather.2.cloned.1.call-update
  8.9 0.0 reduce-scatter.4.cloned.1.call-start
  9.0 0.9 multiply_reduce_fusion
  9.8 0.6 fusion.32
  12.3 0.8 compare_reduce_fusion
  13.0 0.1 pad_add_fusion
  13.1 0.1 broadcast_in_dim.27
  13.2 0.1 iota_add_fusion
  13.3 1.1 compare_and_fusion
  14.4 89.9 %all-gather.2.cloned.1.call-done = bf16[8192,1024]{1,0:T(8,128)(2,1)} async-done(((bf16[512,1024]{1,0:T(8,128)(2,1)}), bf16[8192,1024]{1,0:T(8,128)(2,1)}) %all-gather.2.cloned.1.call-update) | async-done | bytes 16777232 | tf_op jit(solution)/shard_map/all_gather | solution.py:21
  104.4 2.2 dynamic-slice_bitcast_fusion.2
  106.6 2.0 pad_maximum_fusion
  108.7 6.1 %reshape.97 = bf16[1536,2,4,128]{3,2,1,0:T(4,128)(2,1)} reshape(bf16[3,512,1024]{2,1,0:T(8,128)(2,1)} %pad_maximum_fusion) | data formatting | bytes 6291456 | tf_op jit(solution)/shard_map/reshape | solution.py:26
  114.8 3.4 %fusion.31 = (bf16[1536,1,4,128]{3,2,1,0:T(4,128)(2,1)S(1)}, bf16[1536,1,4,128]{3,2,1,0:T(4,128)(2,1)}) fusion(bf16[1536,2,4,128]{3,2,1,0:T(4,128)(2,1)} %reshape.97), kind=kLoop, calls=%fused_computation.36 | loop fusion | bytes 6291456 | tf_op jit(solution)/shard_map/slice | solution.py:28
  118.1 2.3 copy.20
  120.4 0.0 copy-done
  120.4 3.2 %fusion.11 = f32[4,1536,512]{2,1,0:T(8,128)S(1)} fusion(bf16[1536,1,4,128]{3,2,1,0:T(4,128)(2,1)} %get-tuple-element.11, bf16[512,512]{1,0:T(8,128)(2,1)S(1)} %copy-done), kind=kOutput, calls=%fused_computation.17 | convolution fusion | flops 805306368 | bytes 14680064 | tf_op jit(solution)/shard_map/htd,hsd->hts/dot_general | solution.py:36
  123.6 8.1 %fusion.33 = (f32[4,512]{1,0:T(4,128)S(1)}, bf16[4,512,1536]{1,2,0:T(8,128)(2,1)}) fusion(f32[4,1536,512]{2,1,0:T(8,128)S(1)} %fusion.11, pred[512,1536]{0,1:T(8,128)(4,1)S(1)} %compare_and_fusion), kind=kOutput, calls=%fused_computation.38 | output fusion | flops 22021632 | bytes 19668992 | tf_op jit(solution)/shard_map/sub | solution.py:40
  131.7 4.3 %fusion.23 = bf16[512,4,128]{0,2,1:T(8,128)(2,1)S(1)} fusion(bf16[4,512,1536]{1,2,0:T(8,128)(2,1)} %get-tuple-element.16, bf16[1536,1,4,128]{0,3,2,1:T(8,128)(2,1)} %copy.20, f32[512,4]{0,1:T(4,128)S(1)} %bitcast.65), kind=kOutput, calls=%fused_computation.21 | convolution fusion | flops 805830656 | bytes 8396800 | tf_op jit(solution)/shard_map/hts,hsd->htd/dot_general | solution.py:43
  136.0 9.2 %fusion.5 = bf16[7168,512]{0,1:T(8,128)(2,1)} fusion(bf16[512,512]{0,1:T(8,128)(2,1)S(1)} %bitcast.64, bf16[512,7168]{1,0:T(8,128)(2,1)} %param.9), kind=kOutput, calls=%fused_computation.8 | convolution fusion | flops 3761766400 | bytes 15204352 | tf_op jit(solution)/shard_map/dot_general | solution.py:51
  145.2 0.0 copy-start.1
  145.2 10.5 %copy.18 = bf16[7168,512]{1,0:T(8,128)(2,1)} copy(bf16[7168,512]{0,1:T(8,128)(2,1)} %fusion.5) | data formatting | bytes 14680064
  155.7 0.0 reduce-scatter.4.cloned.1.call-update
  155.7 106.8 %reduce-scatter.4.cloned.1.call-done = bf16[896,512]{1,0:T(8,128)(2,1)} async-done(((bf16[7168,512]{1,0:T(8,128)(2,1)}), bf16[896,512]{1,0:T(8,128)(2,1)}) %reduce-scatter.4.cloned.1.call-update) | async-done | bytes 917520
  262.5 2.2 copy.19
  264.7 0.0 copy-done.1
  (3 shorter events, 0.0 us)
Async XLA Ops:
  6.5 113.9 %copy-start = (bf16[512,512]{1,0:T(8,128)(2,1)S(1)}, bf16[512,512]{1,0:T(8,128)(2,1)}, u32[]{:S(2)}) copy-start(bf16[512,512]{1,0:T(8,128)(2,1)} %param.5) | copy-start | bytes 1572868
  6.5 97.9 %all-gather.2.cloned.1.call-start = ((), (), s32[]{:S(2)}) async-start(), calls=%async_computation.1 | async-start | bytes 17825792 | tf_op jit(solution)/shard_map/all_gather | solution.py:21
  8.9 253.6 %reduce-scatter.4.cloned.1.call-start = ((), (), s32[]{:S(2)}) async-start(), calls=%async_computation.2 | async-start | bytes 8257536
  145.2 119.5 %copy-start.1 = (bf16[512,512]{1,0:T(8,128)(2,1)S(1)}, bf16[512,512]{1,0:T(8,128)(2,1)}, u32[]{:S(2)}) copy-start(bf16[512,512]{1,0:T(8,128)(2,1)} %param.5) | copy-start | bytes 1572868
Sparse Core Ops, SparseCore 0:
  9.1 95.2 all-gather.1
  155.8 106.5 reduce-scatter.3
where the time goes:
time: 272 us
  waiting for transfers between devices  197 us (72%)
  local copies, waits for them, and re-layouts  27.4 us (10%)
  matrix products  16.7 us (6%)
  other arithmetic  15.4 us (6%)
  between operations  15.3 us (6%)
    unnamed x3, waiting for transfers between devices  107 us
    all_gather x1, waiting for transfers between devices, per_device(): lax.all_gather(jnp.concatenate([key_rows, value_rows], axis=1), 'ctx', ax...  89.9 us
    unnamed x7, local copies, waits for them, and re-layouts  15 us
    dot_general x1, matrix products, per_device(): lax.dot_general(out_weight, attended, (((0,), (1,)), ((), ())), preferred...  9.24 us
    sub x1, other arithmetic, per_device(): expo = jnp.where(allowed[None], jnp.exp(scores - run_max[..., None]), 0.0)  8.07 us
    reshape x1, local copies, waits for them, and re-layouts, per_device(): picked = jnp.stack([lax.dynamic_slice_in_dim(kv_piece, own_choice[s] * BL...  6.08 us
  transfers between devices with their start and end apart: 2, of which 2 were waited for; matrix products, arithmetic and copies ran while one was open for 1% of the time, Pallas kernels for 0%

commit v1 on v0

--- a/solution.py
+++ b/solution.py
@@ -18,8 +18,14 @@
     query_heads = queries.reshape(row_count, head_count, HD).transpose(1, 0, 2)
     own_choice = lax.dynamic_slice_in_dim(selection, ctx_place, 1, 0)[0]
     usable = jnp.concatenate([jnp.ones((1,), bool), own_choice[1:] != own_choice[0]])
-    kv_piece = lax.all_gather(
-        jnp.concatenate([key_rows, value_rows], axis=1), "ctx", axis=0, tiled=True
+    kv_piece = jnp.concatenate(
+        lax.all_to_all(
+            jnp.stack([jnp.concatenate([key_rows, value_rows], axis=1)] * lax.axis_size("ctx")),
+            "ctx",
+            0,
+            0,
+        ),
+        axis=0,
     )
     picked = jnp.stack(
         [lax.dynamic_slice_in_dim(kv_piece, own_choice[s] * BLOCK, BLOCK, 0) for s in range(topk)]

time: 272 us -> 452 us (1.66)
  waiting for transfers between devices: 197 us -> 364 us
  starting transfers between devices: 0.04 us -> 7.93 us
  local copies, waits for them, and re-layouts: 27.4 us -> 33.4 us
    all_to_all x0 -> x1, waiting for transfers between devices: none -> 253 us  [per_device(): lax.all_to_all(jnp.stack([jnp.concatenate([key_rows, value_rows], axis=1)...]
    all_gather x1 -> x0, waiting for transfers between devices: 89.9 us -> none  [per_device(): lax.all_gather(jnp.concatenate([key_rows, value_rows], axis=1), 'ctx', ax...]
    all_to_all x0 -> x1, starting transfers between devices: none -> 7.89 us  [per_device(): lax.all_to_all(jnp.stack([jnp.concatenate([key_rows, value_rows], axis=1)...]
    another operation x0 -> x1, local copies, waits for them, and re-layouts: none -> 5.99 us  [per_device(): jnp.stack([jnp.concatenate([key_rows, value_rows], axis=1)] * lax.axis_si...]
    unnamed x3 -> x2, waiting for transfers between devices: 107 us -> 111 us
    unnamed x7 -> x9, local copies, waits for them, and re-layouts: 15 us -> 15 us
where the time goes in v1:
time: 452 us; the launch traced here: 451 us
  waiting for transfers between devices  364 us (81%)
  local copies, waits for them, and re-layouts  33.4 us (7%)
  matrix products  16.7 us (4%)
  between operations  15.5 us (3%)
  other arithmetic  13.7 us (3%)
  starting transfers between devices  7.93 us (2%)
    all_to_all x1, waiting for transfers between devices, per_device(): lax.all_to_all(jnp.stack([jnp.concatenate([key_rows, value_rows], axis=1)...  253 us
    unnamed x2, waiting for transfers between devices  111 us
    unnamed x9, local copies, waits for them, and re-layouts  15 us
    dot_general x1, matrix products, per_device(): lax.dot_general(out_weight, attended, (((0,), (1,)), ((), ())), preferred...  9.24 us
  transfers between devices with their start and end apart: 2, of which 2 were waited for; matrix products, arithmetic and copies ran while one was open for 1% of the time, Pallas kernels for 0%

profile of v1, /device:TPU:1, one launch (start us, length us, event | category | flops | bytes accessed | tf_op | source)
XLA Modules:
  0.0 451.1 jit_solution(926638672040405668)
XLA Ops:
  6.5 0.0 copy-start
  6.5 1.4 pad_maximum_fusion.1
  7.9 6.0 %stack.10 = bf16[16,512,1024]{2,1,0:T(8,128)(2,1)} broadcast(bf16[512,1024]{1,0:T(8,128)(2,1)S(1)} %pad_maximum_fusion.1), dimensions={1,2} | broadcast | bytes 17825792 | tf_op jit(solution)/shard_map/stack | solution.py:23
  13.9 0.0 copy-start.2
  13.9 7.9 %all-to-all-start = ((bf16[16,512,1024]{2,1,0:T(8,128)(2,1)}), bf16[16,512,1024]{2,1,0:T(8,128)(2,1)}, u32[]{:S(2)}, u32[]{:S(2)}) async-start(bf16[16,512,1024]{2,1,0:T(8,128)(2,1)} %stack.10), calls=%async_computation | async-start | bytes 33554432 | tf_op jit(solution)/shard_map/all_to_all | solution.py:22
  21.8 0.0 reduce-scatter.4.cloned.1.call-start
  21.8 0.0 copy-done.2
  21.8 0.2 multiply_reduce_fusion
  22.0 0.6 fusion.32
  24.7 0.1 iota_add_fusion
  24.7 0.8 compare_reduce_fusion
  25.5 0.1 pad_add_fusion
  25.6 0.1 broadcast_in_dim.27
  25.7 1.1 compare_and_fusion
  26.8 253.3 %all-to-all-done = bf16[16,512,1024]{2,1,0:T(8,128)(2,1)} async-done(((bf16[16,512,1024]{2,1,0:T(8,128)(2,1)}), bf16[16,512,1024]{2,1,0:T(8,128)(2,1)}, u32[]{:S(2)}, u32[]{:S(2)}) %all-to-all-start) | async-done | bytes 16777248 | tf_op jit(solution)/shard_map/all_to_all | solution.py:22
  280.1 2.2 dynamic-slice_bitcast_fusion.2
  282.4 2.0 pad_maximum_fusion
  284.4 6.1 %reshape.103 = bf16[1536,2,4,128]{3,2,1,0:T(4,128)(2,1)} reshape(bf16[3,512,1024]{2,1,0:T(8,128)(2,1)} %pad_maximum_fusion) | data formatting | bytes 6291456 | tf_op jit(solution)/shard_map/reshape | solution.py:32
  290.5 3.4 fusion.31
  293.9 2.3 copy.20
  296.2 0.0 copy-done
  296.2 3.2 fusion.11
  299.4 8.1 %fusion.33 = (f32[4,512]{1,0:T(4,128)S(1)}, bf16[4,512,1536]{1,2,0:T(8,128)(2,1)}) fusion(f32[4,1536,512]{2,1,0:T(8,128)S(1)} %fusion.11, pred[512,1536]{0,1:T(8,128)(4,1)S(1)} %compare_and_fusion), kind=kOutput, calls=%fused_computation.38 | output fusion | flops 22021632 | bytes 19668992 | tf_op jit(solution)/shard_map/sub | solution.py:46
  307.5 4.3 fusion.23
  311.7 9.2 %fusion.5 = bf16[7168,512]{0,1:T(8,128)(2,1)} fusion(bf16[512,512]{0,1:T(8,128)(2,1)S(1)} %bitcast.65, bf16[512,7168]{1,0:T(8,128)(2,1)} %param.9), kind=kOutput, calls=%fused_computation.8 | convolution fusion | flops 3761766400 | bytes 15204352 | tf_op jit(solution)/shard_map/dot_general | solution.py:57
  321.0 0.0 copy-start.1
  321.0 10.5 %copy.18 = bf16[7168,512]{1,0:T(8,128)(2,1)} copy(bf16[7168,512]{0,1:T(8,128)(2,1)} %fusion.5) | data formatting | bytes 14680064
  331.4 0.0 reduce-scatter.4.cloned.1.call-update
  331.5 110.6 %reduce-scatter.4.cloned.1.call-done = bf16[896,512]{1,0:T(8,128)(2,1)} async-done(((bf16[7168,512]{1,0:T(8,128)(2,1)}), bf16[896,512]{1,0:T(8,128)(2,1)}) %reduce-scatter.4.cloned.1.call-update) | async-done | bytes 917520
  442.1 2.2 copy.19
  444.3 0.0 copy-done.1
  (3 shorter events, 0.0 us)
Async XLA Ops:
  6.5 289.6 %copy-start = (bf16[512,512]{1,0:T(8,128)(2,1)S(1)}, bf16[512,512]{1,0:T(8,128)(2,1)}, u32[]{:S(2)}) copy-start(bf16[512,512]{1,0:T(8,128)(2,1)} %param.5) | copy-start | bytes 1572868
  13.9 7.9 %copy-start.2 = (s32[16,3]{0,1:T(4,128)S(1)}, s32[16,3]{0,1:T(4,128)}, u32[]{:S(2)}) copy-start(s32[16,3]{0,1:T(4,128)} %param.8) | copy-start | bytes 580
  13.9 266.2 %all-to-all-start = ((bf16[16,512,1024]{2,1,0:T(8,128)(2,1)}), bf16[16,512,1024]{2,1,0:T(8,128)(2,1)}, u32[]{:S(2)}, u32[]{:S(2)}) async-start(bf16[16,512,1024]{2,1,0:T(8,128)(2,1)} %stack.10), calls=%async_computation | async-start | bytes 33554432 | tf_op jit(solution)/shard_map/all_to_all | solution.py:22
  21.8 420.3 %reduce-scatter.4.cloned.1.call-start = ((), (), s32[]{:S(2)}) async-start(), calls=%async_computation.2 | async-start | bytes 8257536
  321.0 123.3 %copy-start.1 = (bf16[512,512]{1,0:T(8,128)(2,1)S(1)}, bf16[512,512]{1,0:T(8,128)(2,1)}, u32[]{:S(2)}) copy-start(bf16[512,512]{1,0:T(8,128)(2,1)} %param.5) | copy-start | bytes 1572868
Sparse Core Ops, SparseCore 0:
  331.6 110.4 reduce-scatter.3
